TPU v7x, 512 devices: a whole 4x8x8 slice. The times are simulated.
512 devices in a mesh: dp: 64 (over x, z, y_lo), tensor: 8 (over y_hi, core).
Axes of the slice: x: 4, y: 8 (y_hi: 4, y_lo: 2; y = y_hi * 2 + y_lo), z: 8, core: 2. Of those that a mesh axis runs over, the one named last changes fastest.
Arguments:
- tokens: bfloat16 [16384, 8192], P('dp', 'tensor'), may hold values from -6 to 6
- norm_gain: bfloat16 [8192], P('tensor'), may hold values from 0.099609375 to 1.8984375
- kept_blocks: bfloat16 [8192, 6144], P('dp', 'tensor'), may hold values from -0.09375 to 0.09375
- block_cols: int32 [64, 48], P('dp', 'tensor'), may hold values from 0 to 9, as said below
- row_counts: int32 [64, 8], P('dp', 'tensor'), may hold values from 4 to 6, as said below
Outputs:
- projected: bfloat16 [16384, 10240], P('dp', 'tensor')
Inputs may be any that keep to these rules, and one draw needn't show every extreme that they name: `block_cols`: in each row block the 6 slots of one shard name distinct column blocks of that shard, also the slots beyond row_counts. `row_counts`: in every shard some row block has 6 kept blocks.
All inputs are finite; a program needn't handle non-finite values.
Results may differ from a plain program's by a relative error of at most 0.0049.
Values may be sent and summed in bfloat16 or wider, within the bound.
No kernel may reach another device: no remote copies, remote signals or barrier semaphores. Data moves between devices by JAX's collectives and lax.ppermute only.
A program may use at most 128 MiB of HBM per device.

v0:
```python
import math

import jax
import jax.numpy as jnp
from jax import lax
from jax.sharding import PartitionSpec as P

KVH = 8
GROUP = 8
HD = 128
BS = 128


rope_theta = 500000.0


def rotate(mixed, positions):
    row_count = mixed.shape[0]
    head_view = mixed.reshape(row_count, -1, GROUP + 2, HD)
    half_size = HD // 2
    inverse_freq = rope_theta ** (-(jnp.arange(half_size).astype(jnp.float32) * 2.0 / HD))
    angles = positions[:, None] * inverse_freq[None, :]
    cosine = jnp.cos(angles)[:, None, None, :]
    sine_part = jnp.sin(angles)[:, None, None, :]
    first_half = head_view[..., :half_size]
    second = head_view[..., half_size:]
    turned = jnp.concatenate(
        [first_half * cosine - second * sine_part, second * cosine + first_half * sine_part],
        axis=-1,
    )
    rotated_heads = (jnp.arange(GROUP + 2) < GROUP + 1)[None, None, :, None]
    return jnp.where(rotated_heads, turned, head_view).reshape(row_count, -1)


def per_device(tokens, norm_gain, kept_blocks, block_cols, row_counts):
    tensor_count = lax.axis_size("tensor")
    column_blocks = KVH // tensor_count * (GROUP + 2) * HD // BS
    rows_here = block_cols.shape[0]
    slot_count = block_cols.shape[1]
    gathered, gain_all = (
        lax.all_gather(tokens, "tensor", axis=1, tiled=True),
        lax.all_gather(norm_gain, "tensor", axis=0, tiled=True),
    )
    floats = gathered.astype(jnp.float32)
    mean_square = jnp.mean(floats * floats, axis=-1, keepdims=True)
    normed = (floats * lax.rsqrt(mean_square + 1e-05) * gain_all.astype(jnp.float32)).astype(
        jnp.bfloat16
    )
    filled = jnp.arange(slot_count)[None, :] < row_counts
    placing = (
        (block_cols[:, :, None] == jnp.arange(column_blocks)[None, None, :]) & filled[:, :, None]
    ).astype(jnp.bfloat16)
    stacked = kept_blocks.reshape(rows_here, BS, slot_count * BS)
    initial = jnp.zeros((tokens.shape[0], column_blocks * BS), jnp.float32)
    summed = initial
    block_piece = lax.all_gather(stacked, "dp", axis=0, tiled=True)
    place_piece = lax.all_gather(placing, "dp", axis=0, tiled=True)
    piece_rows = block_piece.shape[0]
    group_size = math.gcd(piece_rows, 8)
    step_count = piece_rows // group_size
    block_groups = block_piece.reshape(step_count, group_size, BS, slot_count * BS)
    place_groups = place_piece.reshape(step_count, group_size, slot_count, column_blocks)

    def advance(running, step_input):
        step_index, block_set, place_set = step_input
        feature_rows = lax.dynamic_slice_in_dim(
            normed, step_index * group_size * BS, group_size * BS, 1
        )
        dense_rows = jnp.einsum(
            "gksj,gsc->gkcj",
            block_set.reshape(group_size, BS, slot_count, BS),
            place_set,
            preferred_element_type=jnp.float32,
        )
        dense_rows = dense_rows.astype(jnp.bfloat16).reshape(group_size * BS, column_blocks * BS)
        return (
            running + jnp.dot(feature_rows, dense_rows, preferred_element_type=jnp.float32),
            None,
        )

    summed, _ = lax.scan(
        advance, summed, (jnp.arange(step_count, dtype=jnp.int32), block_groups, place_groups)
    )
    positions = jnp.arange(tokens.shape[0]).astype(jnp.float32)
    return rotate(summed, positions).astype(jnp.bfloat16)


def solution(mesh):
    in_specs = (
        P("dp", "tensor"),
        P("tensor"),
        P("dp", "tensor"),
        P("dp", "tensor"),
        P("dp", "tensor"),
    )
    out_specs = P("dp", "tensor")
    return jax.shard_map(
        per_device, mesh=mesh, in_specs=in_specs, out_specs=out_specs, check_vma=False
    )
```

profile of v0, /device:TPU:16, one launch (start us, length us, event | category | flops | bytes accessed | tf_op | source)
XLA Modules:
  0.0 536.7 jit_solution(7560243581540151692)
XLA Ops:
  8.0 15.7 %all_gather.13 = bf16[8192]{0:T(1024)(128)(2,1)S(1)} all-gather(bf16[1024]{0:T(1024)(128)(2,1)} %param.8), channel_id=1, replica_groups=mesh['dp'=64,'tensor'=8] {'tensor'}, dimensions={0}, use_global_device_ids=true | all-gather | bytes 18432 | tf_op jit(solution)/shard_map/all_gather | solution.py:42
  25.1 166.4 %all_gather.14 = bf16[64,6,10]{2,1,0:T(8,128)(2,1)S(1)} all-gather(bf16[1,6,10]{2,1,0:T(8,128)(2,1)S(1)} %fusion.12), channel_id=1, replica_groups=mesh['dp'=64,'tensor'=8] {'dp'}, dimensions={0}, use_global_device_ids=true | all-gather | bytes 7800 | tf_op jit(solution)/shard_map/all_gather | solution.py:57
  192.6 3.3 fusion.7
  196.1 3.1 fusion.9
  199.2 216.9 %all-gather.6.cloned.1.call-done = bf16[8192,768]{1,0:T(8,128)(2,1)} async-done(((bf16[128,768]{1,0:T(8,128)(2,1)}), bf16[8192,768]{1,0:T(8,128)(2,1)}) %all-gather.6.cloned.1.call-update) | async-done | bytes 12582928 | tf_op jit(solution)/shard_map/all_gather | solution.py:56
  416.1 111.3 %while.13 = (s32[]{:T(128)}, f32[256,1280]{1,0:T(8,128)S(1)}, s32[8]{0:T(128)S(1)}, bf16[256,8192]{1,0:T(8,128)(2,1)}, bf16[8,8,6,10]{3,2,1,0:T(8,128)(2,1)S(1)}...) while((s32[]{:T(128)}, f32[256,1280]{1,0:T(8,128)S(1)}, ...), condition=%wide.region_2.3_spmd.clone, body=%wide.region_1.2_spmd.clone.sunk | while | flops 688783360 | bytes 21512372 | solution.py:81
  418.9 1.6 copy.35
  420.5 3.1 copy.36
  423.6 2.9 convolution_convert_fusion.2
  426.5 3.5 convolution_add_fusion.2
  432.8 1.6 copy.35
  434.4 3.1 copy.36
  437.5 2.9 convolution_convert_fusion.2
  440.4 3.5 convolution_add_fusion.2
  448.3 3.1 copy.36
  451.4 2.9 convolution_convert_fusion.2
  454.3 3.5 convolution_add_fusion.2
  462.2 3.1 copy.36
  465.3 2.9 convolution_convert_fusion.2
  468.2 3.5 convolution_add_fusion.2
  476.1 3.1 copy.36
  479.2 2.9 convolution_convert_fusion.2
  482.2 3.5 convolution_add_fusion.2
  490.1 3.1 copy.36
  493.2 2.9 convolution_convert_fusion.2
  496.1 3.5 convolution_add_fusion.2
  504.0 3.1 copy.36
  507.1 2.9 convolution_convert_fusion.2
  510.0 3.5 convolution_add_fusion.2
  517.9 3.1 copy.36
  521.0 2.9 convolution_convert_fusion.2
  523.9 3.5 convolution_add_fusion.2
  (49 shorter events, 32.3 us)
Async XLA Ops:
  6.5 186.1 %all-gather.4.cloned.1.call-start = ((), (), s32[]{:S(2)}) async-start(), calls=%async_computation | async-start | bytes 4718592 | tf_op jit(solution)/shard_map/all_gather | solution.py:41
  7.3 408.8 %all-gather.6.cloned.1.call-start = ((), (), s32[]{:S(2)}) async-start(), calls=%async_computation.1 | async-start | bytes 12779520 | tf_op jit(solution)/shard_map/all_gather | solution.py:56
  192.6 3.5 copy-start
  527.5 0.8 copy-start.1
  527.5 0.9 copy-start.2
Sparse Core Ops, SparseCore 0:
  9.5 56.8 all-gather.3
  68.5 347.5 all-gather.5
where the time goes:
time: 538 us; the launch traced here: 537 us
  waiting for transfers between devices  218 us (41%)
  blocking collectives  182 us (34%)
  local copies, waits for them, and re-layouts  56.6 us (11%)
  matrix products  51.5 us (10%)
  between operations  14.1 us (3%)
  other arithmetic  8.57 us (2%)
    all_gather x1, waiting for transfers between devices, per_device(): block_piece = lax.all_gather(stacked, 'dp', axis=0, tiled=True)  217 us
    all_gather x1, blocking collectives, per_device(): place_piece = lax.all_gather(placing, 'dp', axis=0, tiled=True)  166 us
    dynamic_slice x24, local copies, waits for them, and re-layouts, per_device(): lax.scan(advance, summed, (jnp.arange(step_count, dtype=jnp.int32), block...  29.7 us
    dot_general x8, matrix products, advance(): jnp.dot(feature_rows, dense_rows, preferred_element_type=jnp.float32)  28.1 us
    reshape x8, local copies, waits for them, and re-layouts, advance(): block_set.reshape(group_size, BS, slot_count, BS)  24.7 us
    dot_general x8, matrix products, advance(): jnp.einsum('gksj,gsc->gkcj', block_set.reshape(group_size, BS, slot_count...  23.5 us
    all_gather x1, blocking collectives, per_device(): lax.all_gather(norm_gain, 'tensor', axis=0, tiled=True)  15.7 us
  transfers between devices with their start and end apart: 2, of which 1 were waited for; matrix products, arithmetic and copies ran while one was open for 2% of the time, Pallas kernels for 0%

commit v1 on v0

v1 whole, which is shorter than its diff:
```python
import functools

import jax
import jax.numpy as jnp
from jax import lax
from jax.experimental import pallas as pl
from jax.experimental.pallas import tpu as pltpu
from jax.sharding import Mesh
from jax.sharding import PartitionSpec as P

KVH = 8
GROUP = 8
HD = 128
BS = 128
ROWS_PER_STEP = 8

rope_theta = 500000.0

DP = ("x", "z", "ylo")
TP = ("yhi", "core")


def rope_tables(count):
    half_size = HD // 2
    positions = jnp.arange(count).astype(jnp.float32)
    inverse_freq = rope_theta ** (-(jnp.arange(half_size).astype(jnp.float32) * 2.0 / HD))
    angles = positions[:, None] * inverse_freq[None, :]
    cosine = jnp.cos(angles)
    sine_part = jnp.sin(angles)
    return (
        jnp.concatenate([cosine, cosine], axis=1),
        jnp.concatenate([-sine_part, sine_part], axis=1),
    )


def qkv_kernel(heads, slots, steps, dest_ref, normed_ref, w_ref, cos_ref, sin_ref, out_ref, acc_ref):
    step = pl.program_id(0)

    @pl.when(step == 0)
    def _():
        acc_ref[...] = jnp.zeros_like(acc_ref)

    for j in range(ROWS_PER_STEP):
        row = step * ROWS_PER_STEP + j
        y = jnp.dot(
            normed_ref[:, j * BS:(j + 1) * BS],
            w_ref[j * BS:(j + 1) * BS, :],
            preferred_element_type=jnp.float32,
        )
        for s in range(slots):
            d = dest_ref[row * slots + s]
            acc_ref[d] += y[:, s * BS:(s + 1) * BS]

    @pl.when(step == steps - 1)
    def _():
        cos = cos_ref[...]
        sin = sin_ref[...]
        for c in range(heads):
            x = acc_ref[c]
            if c < GROUP + 1:
                x = x * cos + pltpu.roll(x, HD // 2, 1) * sin
            out_ref[:, c * BS:(c + 1) * BS] = x.astype(out_ref.dtype)


def block_sparse_qkv(dest, normed, w, cos, sin, heads, slots):
    tokens = normed.shape[0]
    feature_count = normed.shape[1]
    steps = feature_count // (ROWS_PER_STEP * BS)
    chunk = ROWS_PER_STEP * BS
    kernel = functools.partial(qkv_kernel, heads, slots, steps)
    flops = 2 * tokens * feature_count * slots * BS
    bytes_accessed = normed.size * 2 + w.size * 2 + tokens * heads * BS * 2
    return pl.pallas_call(
        kernel,
        out_shape=jax.ShapeDtypeStruct((tokens, heads * BS), jnp.bfloat16),
        grid_spec=pltpu.PrefetchScalarGridSpec(
            num_scalar_prefetch=1,
            grid=(steps,),
            in_specs=[
                pl.BlockSpec((tokens, chunk), lambda i, d: (0, i)),
                pl.BlockSpec((chunk, slots * BS), lambda i, d: (i, 0)),
                pl.BlockSpec((tokens, HD), lambda i, d: (0, 0)),
                pl.BlockSpec((tokens, HD), lambda i, d: (0, 0)),
            ],
            out_specs=pl.BlockSpec((tokens, heads * BS), lambda i, d: (0, 0)),
            scratch_shapes=[pltpu.VMEM((heads + 1, tokens, BS), jnp.float32)],
        ),
        compiler_params=pltpu.CompilerParams(dimension_semantics=("arbitrary",)),
        cost_estimate=pl.CostEstimate(flops=flops, bytes_accessed=bytes_accessed, transcendentals=0),
    )(dest, normed, w, cos, sin)


def per_device(tokens, norm_gain, kept_blocks, block_cols, row_counts):
    tensor_count = lax.axis_size(TP)
    heads = KVH // tensor_count * (GROUP + 2) * HD // BS
    slots = block_cols.shape[1]

    w = lax.all_gather(kept_blocks, "ylo", axis=0, tiled=True)
    w = lax.all_gather(w, ("x", "z"), axis=0, tiled=True)

    dest_here = jnp.where(jnp.arange(slots)[None, :] < row_counts, block_cols, heads)
    dest = lax.all_gather(dest_here, DP, axis=0, tiled=True).reshape(-1)

    gathered = lax.all_gather(tokens, TP, axis=1, tiled=True)
    gain_all = lax.all_gather(norm_gain, TP, axis=0, tiled=True)
    floats = gathered.astype(jnp.float32)
    mean_square = jnp.mean(floats * floats, axis=-1, keepdims=True)
    normed = (floats * lax.rsqrt(mean_square + 1e-05) * gain_all.astype(jnp.float32)).astype(
        jnp.bfloat16
    )
    cos, sin = rope_tables(tokens.shape[0])
    return block_sparse_qkv(dest, normed, w, cos, sin, heads, slots)


def solution(mesh):
    dp_size = mesh.shape["dp"]
    tp_size = mesh.shape["tensor"]
    fine = Mesh(mesh.devices.reshape(dp_size // 16, 8, 2, tp_size // 2, 2), DP + TP)
    spec = P(DP, TP)
    in_specs = (spec, P(TP), spec, spec, spec)
    return jax.shard_map(per_device, mesh=fine, in_specs=in_specs, out_specs=spec, check_vma=False)
```

time: 538 us -> 231 us (0.43)
  waiting for transfers between devices: 218 us -> 0.73 us
  local copies, waits for them, and re-layouts: 56.6 us -> 1.23 us
  matrix products: 51.5 us -> 0 us
  Pallas kernels: 0 us -> 14.3 us
  blocking collectives: 182 us -> 189 us
    all_gather x2, waiting for transfers between devices: 217 us -> 0.01 us  [the longest x1 0.01 us: per_device(): w = lax.all_gather(w, ('x', 'z'), axis=0, tiled=True)]
    dot_general x16 -> x0, matrix products: 51.5 us -> none  [the longest x8 28.1 us: advance(): jnp.dot(feature_rows, dense_rows, preferred_element_type=jnp.float32)]
    dynamic_slice x24 -> x0, local copies, waits for them, and re-layouts: 29.7 us -> none  [per_device(): lax.scan(advance, summed, (jnp.arange(step_count, dtype=jnp.int32), block...]
    reshape x8 -> x1, local copies, waits for them, and re-layouts: 24.7 us -> 0.72 us  [per_device(): dest = lax.all_gather(dest_here, DP, axis=0, tiled=True).reshape(-1)]
    pallas_call x0 -> x1, Pallas kernels: none -> 14.3 us  [block_sparse_qkv(): pl.pallas_call(kernel, out_shape=jax.ShapeDtypeStruct((tokens, heads * BS...]
    all_gather x2 -> x3, blocking collectives: 182 us -> 189 us  [the longest x1 166 us: per_device(): dest = lax.all_gather(dest_here, DP, axis=0, tiled=True).reshape(-1)]
  transfers between devices with their start and end apart: 2 -> 2, of which waited for: 1 -> 0; matrix products, arithmetic and copies ran while one was open for 2% -> 5% of each run, Pallas kernels for 0% -> 0%
where the time goes in v1:
time: 231 us; the launch traced here: 230 us
  blocking collectives  189 us (82%)
  Pallas kernels  14.3 us (6%)
  between operations  14.1 us (6%)
  other arithmetic  11.2 us (5%)
    all_gather x1, blocking collectives, per_device(): dest = lax.all_gather(dest_here, DP, axis=0, tiled=True).reshape(-1)  166 us
    pallas_call x1, Pallas kernels, block_sparse_qkv(): pl.pallas_call(kernel, out_shape=jax.ShapeDtypeStruct((tokens, heads * BS...  14.3 us
    all_gather x1, blocking collectives, per_device(): gain_all = lax.all_gather(norm_gain, TP, axis=0, tiled=True)  13.6 us
    all_gather x1, blocking collectives, per_device(): w = lax.all_gather(kept_blocks, 'ylo', axis=0, tiled=True)  9.05 us
    convert_element_type x1, other arithmetic, per_device(): (floats * lax.rsqrt(mean_square + 1e-05) * gain_all.astype(jnp.float32))....  5.3 us
  transfers between devices with their start and end apart: 2, of which 0 were waited for; matrix products, arithmetic and copies ran while one was open for 5% of the time, Pallas kernels for 0%

profile of v1, /device:TPU:16, one launch (start us, length us, event | category | flops | bytes accessed | tf_op | source)
XLA Modules:
  0.0 230.4 jit_solution(14808040964269664376)
XLA Ops:
  6.5 0.0 all-gather.4.cloned.1.call-start
  6.5 0.7 all-gather.4.cloned.1.call-update
  7.3 0.0 all-gather.6.cloned.1.call-start
  7.3 9.1 %all_gather.18 = bf16[256,768]{1,0:T(8,128)(2,1)} all-gather(bf16[128,768]{1,0:T(8,128)(2,1)} %param.7), channel_id=1, replica_groups=mesh['x'=4,'z'=8,'ylo'=2,'yhi'=4,'core'=2] {'ylo'}, dimensions={0}, use_global_device_ids=true | all-gather | bytes 589824 | tf_op jit(solution)/shard_map/all_gather | solution.py:98
  16.4 0.0 all-gather.6.cloned.1.call-update
  17.0 13.6 %all_gather.17 = bf16[8192]{0:T(1024)(128)(2,1)S(1)} all-gather(bf16[1024]{0:T(1024)(128)(2,1)} %param.6), channel_id=1, replica_groups=mesh['x'=4,'z'=8,'ylo'=2,'yhi'=4,'core'=2] {'yhi','core'}, dimensions={0}, use_global_device_ids=true | all-gather | bytes 18432 | tf_op jit(solution)/shard_map/all_gather | solution.py:105
  30.6 0.7 fusion.4
  31.3 166.2 %all-gather = s32[64,1,6]{2,1,0:T(1,128)S(1)} all-gather(s32[1,1,6]{2,1,0:T(1,128)S(1)} %fusion.4), channel_id=1, replica_groups=mesh['x'=4,'z'=8,'ylo'=2,'yhi'=4,'core'=2] {'x','z','ylo'}, dimensions={0}, use_global_device_ids=true | all-gather | bytes 1560 | tf_op jit(solution)/shard_map/all_gather | solution.py:102
  197.4 0.5 broadcast.35
  198.0 0.7 reduce.3
  198.7 0.7 reshape.33.dest_ref
  199.4 0.5 fusion.3
  200.0 0.9 pad_maximum_fusion
  200.8 0.0 all-gather.4.cloned.1.call-done
  200.8 3.1 %fusion = f32[256]{0:T(256)S(1)} fusion(bf16[256,8192]{1,0:T(8,128)(2,1)} %all-gather.4.cloned.1.call-done), kind=kLoop, calls=%fused_computation.2 | loop fusion | flops 6291200 | bytes 4195328 | tf_op jit(solution)/shard_map/reduce_sum | solution.py:107
  203.9 5.3 %fusion.2.normed_ref = bf16[256,8192]{1,0:T(8,128)(2,1)} fusion(bf16[256,8192]{1,0:T(8,128)(2,1)} %all-gather.4.cloned.1.call-done, f32[8192]{0:T(1024)S(1)} %convert_element_type.36, f32[256]{0:T(256)S(1)} %add_rsqrt_fusion), kind=kLoop, calls=%fused_computation.4 | loop fusion | flops 8388608 | bytes 8422400 | tf_op jit(solution)/shard_map/convert_element_type | solution.py:108
  209.2 0.0 all-gather.6.cloned.1.call-done.w_ref
  209.2 14.3 %shard_map.55 = bf16[256,1280]{1,0:T(8,128)(2,1)} custom-call(s32[384]{0:T(512)} %reshape.33.dest_ref, bf16[256,8192]{1,0:T(8,128)(2,1)} %fusion.2.normed_ref, bf16[8192,768]{1,0:T(8,128)(2,1)} %all-gather.6.cloned.1.call-done.w_ref, f32[256,128]{1,0:T(8,128)} %get-tuple-element.8.cos_ref, f32[256,128]{1,0:T(8,128)} %get-tuple-element.9.sin_ref), custom_call_target="tpu_custom_call" | custom-call | flops 3221225472 | bytes 17432576 | tf_op jit(solution)/shard_map/pallas_call | solution.py:73
  (4 shorter events, 0.0 us)
Async XLA Ops:
  6.5 194.3 %all-gather.4.cloned.1.call-start = ((), (), s32[]{:S(2)}) async-start(), calls=%async_computation | async-start | bytes 4718592 | tf_op jit(solution)/shard_map/all_gather | solution.py:104
  7.3 202.0 %all-gather.6.cloned.1.call-start = ((), (), s32[]{:S(2)}) async-start(), calls=%async_computation.1 | async-start | bytes 12976128 | tf_op jit(solution)/shard_map/all_gather | solution.py:99
Sparse Core Ops, SparseCore 0:
  9.5 56.0 all-gather.3
  68.7 127.4 all-gather.5

commit v2 on v1

v2 whole, which is shorter than its diff:
```python
import functools

import jax
import jax.numpy as jnp
from jax import lax
from jax.experimental import pallas as pl
from jax.experimental.pallas import tpu as pltpu
from jax.sharding import Mesh
from jax.sharding import PartitionSpec as P

KVH = 8
GROUP = 8
HD = 128
BS = 128
ROWS_PER_STEP = 8

rope_theta = 500000.0

DP = ("x", "z", "ylo")
TP = ("yhi", "core")


def rotate(mixed, positions):
    row_count = mixed.shape[0]
    head_view = mixed.reshape(row_count, -1, GROUP + 2, HD)
    half_size = HD // 2
    inverse_freq = rope_theta ** (-(jnp.arange(half_size).astype(jnp.float32) * 2.0 / HD))
    angles = positions[:, None] * inverse_freq[None, :]
    cosine = jnp.cos(angles)[:, None, None, :]
    sine_part = jnp.sin(angles)[:, None, None, :]
    first_half = head_view[..., :half_size]
    second = head_view[..., half_size:]
    turned = jnp.concatenate(
        [first_half * cosine - second * sine_part, second * cosine + first_half * sine_part],
        axis=-1,
    )
    rotated_heads = (jnp.arange(GROUP + 2) < GROUP + 1)[None, None, :, None]
    return jnp.where(rotated_heads, turned, head_view).reshape(row_count, -1)


def partial_kernel(heads, slots, steps, dest_ref, x_ref, w_ref, out_ref, acc_ref):
    step = pl.program_id(0)

    @pl.when(step == 0)
    def _():
        acc_ref[...] = jnp.zeros_like(acc_ref)

    for j in range(ROWS_PER_STEP):
        row = step * ROWS_PER_STEP + j
        y = jnp.dot(
            x_ref[:, j * BS:(j + 1) * BS],
            w_ref[j * BS:(j + 1) * BS, :],
            preferred_element_type=jnp.float32,
        )
        for s in range(slots):
            d = dest_ref[row * slots + s]
            acc_ref[d] += y[:, s * BS:(s + 1) * BS]

    @pl.when(step == steps - 1)
    def _():
        for c in range(heads):
            out_ref[:, c * BS:(c + 1) * BS] = acc_ref[c]


def block_sparse_partial(dest, x, w, heads, slots):
    tokens, feature_count = x.shape
    steps = feature_count // (ROWS_PER_STEP * BS)
    chunk = ROWS_PER_STEP * BS
    kernel = functools.partial(partial_kernel, heads, slots, steps)
    flops = 2 * tokens * feature_count * slots * BS
    bytes_accessed = x.size * 2 + w.size * 2 + tokens * heads * BS * 4
    return pl.pallas_call(
        kernel,
        out_shape=jax.ShapeDtypeStruct((tokens, heads * BS), jnp.float32),
        grid_spec=pltpu.PrefetchScalarGridSpec(
            num_scalar_prefetch=1,
            grid=(steps,),
            in_specs=[
                pl.BlockSpec((tokens, chunk), lambda i, d: (0, i)),
                pl.BlockSpec((chunk, slots * BS), lambda i, d: (i, 0)),
            ],
            out_specs=pl.BlockSpec((tokens, heads * BS), lambda i, d: (0, 0)),
            scratch_shapes=[pltpu.VMEM((heads + 1, tokens, BS), jnp.float32)],
        ),
        compiler_params=pltpu.CompilerParams(dimension_semantics=("arbitrary",)),
        cost_estimate=pl.CostEstimate(flops=flops, bytes_accessed=bytes_accessed, transcendentals=0),
    )(dest, x, w)


def per_device(tokens, norm_gain, kept_blocks, block_cols, row_counts):
    tensor_count = lax.axis_size(TP)
    heads = KVH // tensor_count * (GROUP + 2) * HD // BS
    slots = block_cols.shape[1]
    pair = lax.axis_size("ylo")
    swap = [(i, (i + 1) % pair) for i in range(pair)]
    half = lax.axis_index("ylo")
    token_count = tokens.shape[0]

    w = lax.all_gather(kept_blocks, ("x", "z"), axis=0, tiled=True)
    dest_here = jnp.where(jnp.arange(slots)[None, :] < row_counts, block_cols, heads)
    dest = lax.all_gather(dest_here, ("x", "z"), axis=0, tiled=True).reshape(-1)

    gathered = lax.all_gather(tokens, TP, axis=1, tiled=True)
    gain_all = lax.all_gather(norm_gain, TP, axis=0, tiled=True)
    floats = gathered.astype(jnp.float32)
    mean_square = jnp.mean(floats * floats, axis=-1, keepdims=True)
    normed = (floats * lax.rsqrt(mean_square + 1e-05) * gain_all.astype(jnp.float32)).astype(
        jnp.bfloat16
    )
    by_half = normed.reshape(token_count, -1, pair, BS)
    mine = lax.dynamic_index_in_dim(by_half, half, 2, keepdims=False).reshape(token_count, -1)
    theirs = lax.dynamic_index_in_dim(by_half, 1 - half, 2, keepdims=False).reshape(token_count, -1)
    received = lax.ppermute(theirs, "ylo", swap)
    x = jnp.concatenate([mine, received], axis=0)

    partial = block_sparse_partial(dest, x, w, heads, slots)
    returned = lax.ppermute(partial[token_count:], "ylo", swap)
    mixed = partial[:token_count] + returned
    positions = jnp.arange(token_count).astype(jnp.float32)
    return rotate(mixed, positions).astype(jnp.bfloat16)


def solution(mesh):
    dp_size = mesh.shape["dp"]
    tp_size = mesh.shape["tensor"]
    fine = Mesh(mesh.devices.reshape(dp_size // 16, 8, 2, tp_size // 2, 2), DP + TP)
    spec = P(DP, TP)
    in_specs = (spec, P(TP), spec, spec, spec)
    return jax.shard_map(per_device, mesh=fine, in_specs=in_specs, out_specs=spec, check_vma=False)
```

time: 231 us -> 224 us (0.970)
  the two profiles are of different devices: /device:TPU:16 before, /device:TPU:2 now
where the time goes in v2:
time: 224 us
  waiting for transfers between devices  70.8 us (32%)
  blocking collectives  58.4 us (26%)
  local copies, waits for them, and re-layouts  40.8 us (18%)
  other arithmetic  14.3 us (6%)
  between operations  14.2 us (6%)
  Pallas kernels  13.8 us (6%)
  starting transfers between devices  11.3 us (5%)
    all_gather x1, blocking collectives, per_device(): dest = lax.all_gather(dest_here, ('x', 'z'), axis=0, tiled=True).reshape(-1)  41.3 us
    all_gather x1, waiting for transfers between devices, per_device(): gathered = lax.all_gather(tokens, TP, axis=1, tiled=True)  39.8 us
    ppermute x1, waiting for transfers between devices, per_device(): returned = lax.ppermute(partial[token_count:], 'ylo', swap)  28.1 us
    dynamic_slice x1, local copies, waits for them, and re-layouts, per_device(): lax.dynamic_index_in_dim(by_half, half, 2, keepdims=False)  26.3 us
    all_gather x1, blocking collectives, per_device(): gain_all = lax.all_gather(norm_gain, TP, axis=0, tiled=True)  17.1 us
    pallas_call x1, Pallas kernels, block_sparse_partial(): pl.pallas_call(kernel, out_shape=jax.ShapeDtypeStruct((tokens, heads * BS...  13.8 us
    reshape x1, local copies, waits for them, and re-layouts, per_device(): by_half = normed.reshape(token_count, -1, pair, BS)  7.72 us
    ppermute x1, starting transfers between devices, per_device(): received = lax.ppermute(theirs, 'ylo', swap)  7.58 us
  transfers between devices with their start and end apart: 4, of which 3 were waited for; matrix products, arithmetic and copies ran while one was open for 22% of the time, Pallas kernels for 0%

profile of v2, /device:TPU:2, one launch (start us, length us, event | category | flops | bytes accessed | tf_op | source)
XLA Modules:
  0.0 223.6 jit_solution(12040189145511179257)
XLA Ops:
  6.5 0.0 all-gather.4.cloned.1.call-start
  6.5 0.7 all-gather.4.cloned.1.call-update
  7.3 0.0 all-gather.6.cloned.1.call-start
  7.3 0.7 all-gather.6.cloned.1.call-update
  8.0 17.1 %all_gather.14 = bf16[8192]{0:T(1024)(128)(2,1)S(1)} all-gather(bf16[1024]{0:T(1024)(128)(2,1)} %param.6), channel_id=1, replica_groups=mesh['x'=4,'z'=8,'ylo'=2,'yhi'=4,'core'=2] {'yhi','core'}, dimensions={0}, use_global_device_ids=true | all-gather | bytes 18432 | tf_op jit(solution)/shard_map/all_gather | solution.py:104
  25.1 39.8 %all-gather.4.cloned.1.call-done = bf16[256,8192]{1,0:T(8,128)(2,1)} async-done(((bf16[256,1024]{1,0:T(8,128)(2,1)}), bf16[256,8192]{1,0:T(8,128)(2,1)}) %all-gather.4.cloned.1.call-update) | async-done | bytes 4194320 | tf_op jit(solution)/shard_map/all_gather | solution.py:103
  64.9 3.3 %fusion = f32[256]{0:T(256)S(1)} fusion(bf16[256,8192]{1,0:T(8,128)(2,1)} %all-gather.4.cloned.1.call-done), kind=kLoop, calls=%fused_computation.2 | loop fusion | flops 6291200 | bytes 4195328 | tf_op jit(solution)/shard_map/reduce_sum | solution.py:106
  68.2 0.2 copy-done
  68.4 3.2 %fusion.2 = bf16[256,8192]{1,0:T(8,128)(2,1)} fusion(bf16[256,8192]{1,0:T(8,128)(2,1)S(1)} %copy-done, f32[8192]{0:T(1024)S(1)} %convert_element_type.39, f32[256]{0:T(256)S(1)} %add_rsqrt_fusion), kind=kLoop, calls=%fused_computation.4 | loop fusion | flops 8388608 | bytes 8422400 | tf_op jit(solution)/shard_map/convert_element_type | solution.py:107
  71.6 7.7 %reshape.117 = bf16[256,32,2,128]{3,2,1,0:T(2,128)(2,1)} reshape(bf16[256,8192]{1,0:T(8,128)(2,1)} %fusion.2) | data formatting | bytes 8388608 | tf_op jit(solution)/shard_map/reshape | solution.py:110
  79.3 26.3 %dynamic-slice_reduce_fusion.1 = (bf16[256,32,128]{2,1,0:T(8,128)(2,1)S(1)}, bf16[256,32,128]{2,1,0:T(8,128)(2,1)S(1)}) fusion(bf16[256,32,2,128]{3,2,1,0:T(2,128)(2,1)} %reshape.117, s32[]{:T(128)S(6)} %select_n.19, s32[]{:T(128)S(6)} %select_n.20), kind=kLoop, calls=%fused_computation.7 | loop fusion | bytes 8388616 | tf_op jit(solution)/shard_map/jit(dynamic_index_in_dim)/dynamic_slice | solution.py:111
  105.6 0.0 copy-start.1
  105.6 2.3 %copy.22 = bf16[32,8,32,128]{3,1,2,0:T(8,128)(2,1)} copy(bf16[32,8,32,128]{3,2,1,0:T(8,128)(2,1)S(1)} %bitcast.17) | data formatting | bytes 4194304
  107.9 7.6 %collective-permute-start = (bf16[256,4096]{1,0:T(8,128)(2,1)}, bf16[256,4096]{1,0:T(8,128)(2,1)}, u32[]{:S(2)}, u32[]{:S(2)}) collective-permute-start(bf16[256,4096]{1,0:T(8,128)(2,1)} %bitcast.13), channel_id=1, source_target_pairs={{0,8},{8,0},{1,9},{9,1},{2,10},{10,2},{3,11},{11,3},{4,12},{12,4},... | collective-permute-start | bytes 6291464 | tf_op jit(solution)/shard_map/ppermute | solution.py:113
  116.2 41.3 %all-gather = s32[32,1,6]{2,1,0:T(1,128)S(1)} all-gather(s32[1,1,6]{2,1,0:T(1,128)S(1)} %fusion.3), channel_id=1, replica_groups=mesh['x'=4,'z'=8,'ylo'=2,'yhi'=4,'core'=2] {'x','z'}, dimensions={0}, use_global_device_ids=true | all-gather | bytes 792 | tf_op jit(solution)/shard_map/all_gather | solution.py:101
  157.5 0.5 broadcast.83
  158.0 0.7 reduce.7
  158.7 0.7 reshape.116.dest_ref
  159.4 1.0 copy.23
  160.4 1.5 collective-permute-done
  161.9 4.1 %pad_maximum_fusion.x_ref = bf16[512,4096]{1,0:T(8,128)(2,1)} fusion(bf16[256,4096]{1,0:T(8,128)(2,1)} %collective-permute-done, bf16[256,4096]{1,0:T(8,128)(2,1)S(1)} %bitcast.18), kind=kLoop, calls=%fused_computation.5 | loop fusion | flops 8388608 | bytes 8388608 | tf_op jit(solution)/shard_map/concatenate | solution.py:114
  166.0 13.8 %shard_map.55 = f32[512,1280]{1,0:T(8,128)} custom-call(s32[192]{0:T(256)} %reshape.116.dest_ref, bf16[512,4096]{1,0:T(8,128)(2,1)} %pad_maximum_fusion.x_ref, bf16[4096,768]{1,0:T(8,128)(2,1)} %all-gather.6.cloned.1.call-done.w_ref), custom_call_target="tpu_custom_call" | custom-call | flops 3221225472 | bytes 13107200 | tf_op jit(solution)/shard_map/pallas_call | solution.py:72
  179.8 1.4 slice.17
  181.2 3.6 %collective-permute-start.1 = (f32[256,1280]{1,0:T(8,128)S(1)}, f32[256,1280]{1,0:T(8,128)S(1)}, u32[]{:S(2)}, u32[]{:S(2)}) collective-permute-start(f32[256,1280]{1,0:T(8,128)S(1)} %slice.17), channel_id=1, source_target_pairs={{0,8},{8,0},{1,9},{9,1},{2,10},{10,2},{3,11},{11,3},{4,12},{12,4},... | collective-permute-start | bytes 3932168 | tf_op jit(solution)/shard_map/ppermute | solution.py:117
  184.9 0.1 broadcast_bitcast_fusion
  185.0 0.3 multiply_cosine_fusion
  185.3 28.1 %collective-permute-done.1 = f32[256,1280]{1,0:T(8,128)S(1)} collective-permute-done((f32[256,1280]{1,0:T(8,128)S(1)}, f32[256,1280]{1,0:T(8,128)S(1)}, u32[]{:S(2)}, u32[]{:S(2)}) %collective-permute-start.1) | collective-permute-done | bytes 1310752 | tf_op jit(solution)/shard_map/ppermute | solution.py:117
  213.4 1.5 slice_add_fusion
  214.9 0.4 copy.14
  215.3 0.2 multiply_subtract_fusion
  215.5 0.2 copy.15
  215.8 1.0 select_convert_fusion
  (10 shorter events, 0.1 us)
Async XLA Ops:
  6.5 58.4 %all-gather.4.cloned.1.call-start = ((), (), s32[]{:S(2)}) async-start(), calls=%async_computation | async-start | bytes 4718592 | tf_op jit(solution)/shard_map/all_gather | solution.py:103
  7.3 158.7 %all-gather.6.cloned.1.call-start = ((), (), s32[]{:S(2)}) async-start(), calls=%async_computation.1 | async-start | bytes 6488064 | tf_op jit(solution)/shard_map/all_gather | solution.py:99
  64.9 3.4 %copy-start = (bf16[256,8192]{1,0:T(8,128)(2,1)S(1)}, bf16[256,8192]{1,0:T(8,128)(2,1)}, u32[]{:S(2)}) copy-start(bf16[256,8192]{1,0:T(8,128)(2,1)} %all-gather.4.cloned.1.call-done) | copy-start | bytes 12582916
  105.6 10.6 %copy-start.1 = (s32[1,6]{1,0:T(1,128)S(1)}, s32[1,6]{1,0:T(1,128)}, u32[]{:S(2)}) copy-start(s32[1,6]{1,0:T(1,128)} %param.8) | copy-start | bytes 76
  107.9 53.9 %collective-permute-start = (bf16[256,4096]{1,0:T(8,128)(2,1)}, bf16[256,4096]{1,0:T(8,128)(2,1)}, u32[]{:S(2)}, u32[]{:S(2)}) collective-permute-start(bf16[256,4096]{1,0:T(8,128)(2,1)} %bitcast.13), channel_id=1, source_target_pairs={{0,8},{8,0},{1,9},{9,1},{2,10},{10,2},{3,11},{11,3},{4,12},{12,4},... | collective-permute-start | bytes 6291464 | tf_op jit(solution)/shard_map/ppermute | solution.py:113
  181.2 32.2 %collective-permute-start.1 = (f32[256,1280]{1,0:T(8,128)S(1)}, f32[256,1280]{1,0:T(8,128)S(1)}, u32[]{:S(2)}, u32[]{:S(2)}) collective-permute-start(f32[256,1280]{1,0:T(8,128)S(1)} %slice.17), channel_id=1, source_target_pairs={{0,8},{8,0},{1,9},{9,1},{2,10},{10,2},{3,11},{11,3},{4,12},{12,4},... | collective-permute-start | bytes 3932168 | tf_op jit(solution)/shard_map/ppermute | solution.py:117
Sparse Core Ops, SparseCore 0:
  9.5 55.3 all-gather.3
  68.1 96.1 all-gather.5
